TPU v7x, 32 devices: a whole 2x2x4 slice. The times are simulated.
32 devices in a mesh: tm: 2 (over x), prow: 4 (over z), pcol: 4 (over y, core).
Axes of the slice: x: 2, y: 2, z: 4, core: 2. Of those that a mesh axis runs over, the one named last changes fastest.
Arguments:
- signal: bfloat16 [2048, 15360], P(('prow', 'pcol'), 'tm'), may hold values from -8 to 8
- offsets: int32 [4], replicated, may hold values from 0 to 511, as said below
- pair_list: int32 [4, 4, 4, 2], P('prow', 'pcol'), may hold values from 0 to 3, as said below
Outputs:
- correlations: bfloat16 [4, 4, 4, 128, 128, 256], P('prow', 'pcol', None, 'tm')
Inputs may be any that keep to these rules, and one draw needn't show every extreme that they name: `offsets`: some window has the largest offset. `pair_list`: entry (a, b) of cell (r, c) pairs row block r n + a with column block b n + c, n the number of devices of pcol, and the row block's number is never above the column block's; pairs may repeat.
All inputs are finite; a program needn't handle non-finite values.
Results may differ from a plain program's by a relative error of at most 0.0058.
Values may be sent and summed in bfloat16 or wider, within the bound.
No kernel may reach another device: no remote copies, remote signals or barrier semaphores. Data moves between devices by JAX's collectives and lax.ppermute only.
A program may use at most 128 MiB of HBM per device.

v0:
```python
import math
import jax
import jax.numpy as jnp
from jax import lax
from jax.sharding import PartitionSpec as P

WIN = 7680
NF = 384
K0 = 32
LAGS = 256
SPAN = 4
NP = 4
STEP = 3840
HALO = 4352
two_pi = 2.0 * math.pi


def from_behind(value, axis, steps):
    count = lax.axis_size(axis)
    initial, last = (max(0, -steps), min(count, count - steps))
    return lax.ppermute(value, axis, [(source, source + steps) for source in range(initial, last)])


def forward_table():
    coarse = 128
    n_coarse = WIN // coarse
    freq_bins = K0 + jnp.arange(NF, dtype=jnp.int32)
    scale = two_pi / WIN
    high_idx = (jnp.arange(n_coarse, dtype=jnp.int32) * coarse)[:, None] * freq_bins[None, :] % WIN
    low_idx = jnp.arange(coarse, dtype=jnp.int32)[:, None] * freq_bins[None, :] % WIN
    high_angle = high_idx.astype(jnp.float32) * scale
    low_angle = low_idx.astype(jnp.float32) * scale
    high_cos, high_sin = (jnp.cos(high_angle)[:, None, :], jnp.sin(high_angle)[:, None, :])
    low_cos, low_sin = (jnp.cos(low_angle)[None], jnp.sin(low_angle)[None])
    cos_full = (high_cos * low_cos - high_sin * low_sin).reshape(WIN, NF)
    sin_full = (high_sin * low_cos + high_cos * low_sin).reshape(WIN, NF)
    sample_idx = jnp.arange(WIN, dtype=jnp.int32)
    taper_curve = 0.5 - 0.5 * jnp.cos(sample_idx.astype(jnp.float32) * (two_pi / WIN))
    cosine = taper_curve[:, None] * cos_full
    sine = -taper_curve[:, None] * sin_full
    return jnp.concatenate([cosine, sine], axis=1).astype(jnp.bfloat16)


def lag_table(count):
    freq_bins = K0 + jnp.arange(NF, dtype=jnp.int32)
    shifted = (jnp.arange(LAGS, dtype=jnp.int32) - LAGS // 2) % WIN
    wrapped = freq_bins[:, None] * shifted[None, :] % WIN
    phase_angle = wrapped.astype(jnp.float32) * (two_pi / WIN)
    factor = 1.0 / math.sqrt(NF * count)
    return jnp.concatenate(
        [jnp.cos(phase_angle) * factor, -jnp.sin(phase_angle) * factor], axis=0
    ).astype(jnp.bfloat16)


def whiten(spectra):
    real_part = spectra[..., :NF]
    imag_part = spectra[..., NF:]
    power_sum = real_part * real_part + imag_part * imag_part
    freq_bins = jnp.arange(NF, dtype=jnp.int32)
    band_matrix = (jnp.abs(freq_bins[:, None] - freq_bins[None, :]) <= SPAN).astype(jnp.float32)
    smooth = jnp.einsum(
        "...f,fg->...g", power_sum, band_matrix, precision=lax.Precision.HIGHEST
    ) / (2 * SPAN + 1)
    water_level = jnp.mean(power_sum, axis=-1, keepdims=True)
    weight = lax.rsqrt(smooth + 0.5 * water_level + 1e-06)
    return (spectra * jnp.concatenate([weight, weight], axis=-1)).astype(jnp.bfloat16)


def cross_pair(row_block, col_block, lags):
    row_real = row_block[..., :NF].astype(jnp.float32)[:, :, None, :]
    row_imag = row_block[..., NF:].astype(jnp.float32)[:, :, None, :]
    col_real = col_block[..., :NF].astype(jnp.float32)[:, None, :, :]
    col_imag = col_block[..., NF:].astype(jnp.float32)[:, None, :, :]
    real_sum = jnp.sum(row_real * col_real + row_imag * col_imag, axis=0)
    imag_sum = jnp.sum(row_imag * col_real - row_real * col_imag, axis=0)
    cross = jnp.concatenate([real_sum, imag_sum], axis=-1).astype(jnp.bfloat16)
    flat = cross.reshape(-1, 2 * NF)
    result = jnp.dot(flat, lags, preferred_element_type=jnp.float32).astype(jnp.bfloat16)
    return result.reshape(row_block.shape[1], col_block.shape[1], LAGS)


def on_device(signal, offsets, pair_list):
    channels_here = signal.shape[0]
    samples_here = signal.shape[1]
    w_dev = samples_here // STEP
    n_tm = lax.axis_size("tm")
    tm_index = lax.axis_index("tm")
    dft_table = forward_table()
    head_samples = signal[:, :HALO]
    next_head = from_behind(head_samples, "tm", -1)
    extended = jnp.concatenate([signal, next_head], axis=1)

    def one_window(window):
        first_sample = window * STEP + offsets[tm_index * w_dev + window]
        segment = lax.dynamic_slice_in_dim(extended, first_sample, WIN, 1)
        return jnp.dot(segment, dft_table, preferred_element_type=jnp.float32)

    spectra = lax.map(one_window, jnp.arange(w_dev, dtype=jnp.int32))
    whitened = whiten(spectra)
    own_piece = whitened[None]
    row_gathered = lax.all_gather(own_piece, ("tm", "pcol"), axis=0, tiled=True)
    col_gathered = lax.all_gather(own_piece, ("tm", "prow"), axis=0, tiled=True)
    row_gathered = row_gathered.reshape(n_tm, -1, w_dev, channels_here, 2 * NF)
    col_gathered = col_gathered.reshape(n_tm, -1, w_dev, channels_here, 2 * NF)
    pick_dim = 1
    lags = lag_table(n_tm * w_dev)
    local_pairs = pair_list[0, 0]
    half_rows = channels_here // n_tm
    first_row = tm_index * half_rows

    def one_pair(pair_index):
        row_pick = local_pairs[pair_index, 0]
        col_pick = local_pairs[pair_index, 1]
        row_whole = lax.dynamic_index_in_dim(row_gathered, row_pick, pick_dim, keepdims=False)
        col_whole = lax.dynamic_index_in_dim(col_gathered, col_pick, pick_dim, keepdims=False)
        row_whole = row_whole.reshape(n_tm * w_dev, channels_here, 2 * NF)
        col_whole = col_whole.reshape(n_tm * w_dev, channels_here, 2 * NF)
        row_block = lax.dynamic_slice_in_dim(row_whole, first_row, half_rows, 1)
        return cross_pair(row_block, col_whole, lags)

    result = lax.map(one_pair, jnp.arange(NP, dtype=jnp.int32))
    return result.reshape(1, 1, NP, half_rows, channels_here, LAGS)


def solution(mesh):
    placed = (P(("prow", "pcol"), "tm"), P(), P("prow", "pcol", None, None))
    return jax.shard_map(
        on_device,
        mesh=mesh,
        in_specs=placed,
        out_specs=P("prow", "pcol", None, "tm", None, None),
        check_vma=False,
    )
```

profile of v0, /device:TPU:0, one launch (start us, length us, event | category | flops | bytes accessed | tf_op | source)
XLA Modules:
  0.0 346.1 jit_solution(10284323201007066720)
XLA Ops:
  10.8 11.8 %multiply_subtract_fusion = (f32[60,128,384]{2,1,0:T(8,128)}, f32[60,128,384]{2,1,0:T(8,128)}) fusion(f32[128,384]{1,0:T(8,128)S(1)} %get-tuple-element.241, f32[60,384]{1,0:T(8,128)S(1)} %get-tuple-element.239, f32[128,384]{1,0:T(8,128)S(1)} %get-tuple-element.240, f32[60,384]{1,0:T(8,128)S(1)} %get-tuple-element.238), kind=kLoop, calls=%fused_computation.28 | loop fusion | flops 17694720 | bytes 24170496 | tf_op jit(solution)/shard_map/sub | solution.py:35
  22.6 9.4 %fusion.17 = (bf16[7680,384]{1,0:T(8,128)(2,1)S(1)}, bf16[7680,384]{1,0:T(8,128)(2,1)S(1)}) fusion(f32[60,128,384]{2,1,0:T(8,128)} %get-tuple-element.235, f32[7680]{0:T(1024)S(1)} %fusion.46, f32[60,128,384]{2,1,0:T(8,128)} %get-tuple-element.234, f32[7680]{0:T(1024)S(1)} %multiply_subtract_fusion.1), kind=kLoop, calls=%fused_computation.24 | loop fusion | flops 11796480 | bytes 35450880 | tf_op jit(solution)/shard_map/convert.7
  32.0 5.0 %pad_maximum_fusion = bf16[7680,768]{1,0:T(8,128)(2,1)} fusion(bf16[7680,384]{1,0:T(8,128)(2,1)S(1)} %get-tuple-element.242, bf16[7680,384]{1,0:T(8,128)(2,1)S(1)} %get-tuple-element.243), kind=kLoop, calls=%fused_computation.22 | loop fusion | flops 23592960 | bytes 23592960 | tf_op jit(solution)/shard_map/concatenate | solution.py:41
  38.4 19.9 %while.24 = (s32[]{:T(128)}, f32[2,128,768]{2,1,0:T(8,128)}, s32[2]{0:T(128)S(1)}, s32[]{:T(128)}, s32[4]{0:T(128)S(1)}, /*index=5*/bf16[128,12032]{1,0:T(8,128)...) while((s32[]{:T(128)}, f32[2,128,768]{2,1,0:T(8,128)}, ...), condition=%wide.region_1.2_spmd, body=%wide.region_0.1_spmd.sunk | while | flops 1509949440 | bytes 14156537 | solution.py:98
  41.4 7.0 %fusion.58 = f32[2,128,768]{2,1,0:T(8,128)} fusion(f32[2,128,768]{2,1,0:T(8,128)} %get-tuple-element.369, s32[]{:T(128)} %get-tuple-element.368, bf16[7680,768]{1,0:T(8,128)(2,1)} %get-tuple-element.386, bf16[128,12032]{1,0:T(8,128)(2,1)S(1)} %get-tuple-element.385, s32[]{:T(128)S(6)} %select_n.122), kind=kOutput, calls=%fused_computation.3.clone.1 | convolution fusion | flops 1509949440 | bytes 14156292 | tf_op jit(solution)/shard_map/while/body/eval_jaxpr/dot_general | solution.py:96
  51.4 7.0 %fusion.58 = f32[2,128,768]{2,1,0:T(8,128)} fusion(f32[2,128,768]{2,1,0:T(8,128)} %get-tuple-element.369, s32[]{:T(128)} %get-tuple-element.368, bf16[7680,768]{1,0:T(8,128)(2,1)} %get-tuple-element.386, bf16[128,12032]{1,0:T(8,128)(2,1)S(1)} %get-tuple-element.385, s32[]{:T(128)S(6)} %select_n.122), kind=kOutput, calls=%fused_computation.3.clone.1 | convolution fusion | flops 1509949440 | bytes 14156292 | tf_op jit(solution)/shard_map/while/body/eval_jaxpr/dot_general | solution.py:96
  59.6 1.7 fusion.21
  61.3 2.0 fusion.22
  64.1 2.0 multiply_convert_fusion.1
  66.1 34.4 %all-gather.5.cloned.1.call-done = bf16[16,128,768]{2,1,0:T(8,128)(2,1)} async-done(((bf16[2,128,768]{2,1,0:T(8,128)(2,1)}), bf16[16,128,768]{2,1,0:T(8,128)(2,1)}) %all-gather.5.cloned.1.call-update) | async-done | bytes 3145744 | tf_op jit(solution)/shard_map/all_gather | solution.py:101
  100.5 62.1 %all-gather.7.cloned.1.call-done = bf16[16,128,768]{2,1,0:T(8,128)(2,1)} async-done(((bf16[2,128,768]{2,1,0:T(8,128)(2,1)}), bf16[16,128,768]{2,1,0:T(8,128)(2,1)}) %all-gather.7.cloned.1.call-update) | async-done | bytes 3145744 | tf_op jit(solution)/shard_map/all_gather | solution.py:102
  162.6 176.7 %while.25 = (s32[]{:T(128)}, bf16[4,64,128,256]{3,2,1,0:T(8,128)(2,1)}, s32[4]{0:T(128)S(1)}, s32[4,2]{0,1:T(2,128)S(1)}, bf16[2,4,2,128,768]{4,3,2,1,0:T(8,128)...) while((s32[]{:T(128)}, ...), condition=%wide.region_6.7_spmd, body=%wide.region_3.6_spmd.sunk | while | flops 3343450112 | bytes 47186712 | solution.py:121
  171.5 29.1 %add_reduce_fusion.2 = (bf16[64,128,384]{2,1,0:T(8,128)(2,1)S(1)}, bf16[64,128,384]{2,1,0:T(8,128)(2,1)S(1)}) fusion(f32[4,128,384]{2,1,0:T(8,128)S(1)} %get-tuple-element.349, f32[4,64,384]{2,1,0:T(8,128)S(1)} %get-tuple-element.351, f32[4,128,384]{2,1,0:T(8,128)S(1)} %get-tuple-element.352, f32[4,64,384]{2,1,0:T(8,128)S(1)} %get-tuple-element.353), kind=kLoop, calls=%fused_computation.6.clone.1 | loop fusion | flops 94371840 | bytes 14942208 | tf_op jit(solution)/shard_map/while/body/eval_jaxpr/reduce_sum | solution.py:74
  200.6 3.9 %fusion.61 = bf16[8192,256]{1,0:T(8,128)(2,1)S(1)} fusion(bf16[768,256]{1,0:T(8,128)(2,1)S(1)} %get-tuple-element.423, bf16[8192,384]{1,0:T(8,128)(2,1)S(1)} %bitcast.62, bf16[8192,384]{1,0:T(8,128)(2,1)S(1)} %bitcast.61), kind=kOutput, calls=%fused_computation.11.clone.1 | convolution fusion | flops 3248488448 | bytes 17170432 | tf_op jit(solution)/shard_map/while/body/eval_jaxpr/dot_general | solution.py:78
  204.5 2.3 constant_dynamic-update-slice_fusion.2
  215.6 29.1 %add_reduce_fusion.2 = (bf16[64,128,384]{2,1,0:T(8,128)(2,1)S(1)}, bf16[64,128,384]{2,1,0:T(8,128)(2,1)S(1)}) fusion(f32[4,128,384]{2,1,0:T(8,128)S(1)} %get-tuple-element.349, f32[4,64,384]{2,1,0:T(8,128)S(1)} %get-tuple-element.351, f32[4,128,384]{2,1,0:T(8,128)S(1)} %get-tuple-element.352, f32[4,64,384]{2,1,0:T(8,128)S(1)} %get-tuple-element.353), kind=kLoop, calls=%fused_computation.6.clone.1 | loop fusion | flops 94371840 | bytes 14942208 | tf_op jit(solution)/shard_map/while/body/eval_jaxpr/reduce_sum | solution.py:74
  244.7 3.9 %fusion.61 = bf16[8192,256]{1,0:T(8,128)(2,1)S(1)} fusion(bf16[768,256]{1,0:T(8,128)(2,1)S(1)} %get-tuple-element.423, bf16[8192,384]{1,0:T(8,128)(2,1)S(1)} %bitcast.62, bf16[8192,384]{1,0:T(8,128)(2,1)S(1)} %bitcast.61), kind=kOutput, calls=%fused_computation.11.clone.1 | convolution fusion | flops 3248488448 | bytes 17170432 | tf_op jit(solution)/shard_map/while/body/eval_jaxpr/dot_general | solution.py:78
  248.7 2.3 constant_dynamic-update-slice_fusion.2
  259.8 29.1 %add_reduce_fusion.2 = (bf16[64,128,384]{2,1,0:T(8,128)(2,1)S(1)}, bf16[64,128,384]{2,1,0:T(8,128)(2,1)S(1)}) fusion(f32[4,128,384]{2,1,0:T(8,128)S(1)} %get-tuple-element.349, f32[4,64,384]{2,1,0:T(8,128)S(1)} %get-tuple-element.351, f32[4,128,384]{2,1,0:T(8,128)S(1)} %get-tuple-element.352, f32[4,64,384]{2,1,0:T(8,128)S(1)} %get-tuple-element.353), kind=kLoop, calls=%fused_computation.6.clone.1 | loop fusion | flops 94371840 | bytes 14942208 | tf_op jit(solution)/shard_map/while/body/eval_jaxpr/reduce_sum | solution.py:74
  288.9 3.9 %fusion.61 = bf16[8192,256]{1,0:T(8,128)(2,1)S(1)} fusion(bf16[768,256]{1,0:T(8,128)(2,1)S(1)} %get-tuple-element.423, bf16[8192,384]{1,0:T(8,128)(2,1)S(1)} %bitcast.62, bf16[8192,384]{1,0:T(8,128)(2,1)S(1)} %bitcast.61), kind=kOutput, calls=%fused_computation.11.clone.1 | convolution fusion | flops 3248488448 | bytes 17170432 | tf_op jit(solution)/shard_map/while/body/eval_jaxpr/dot_general | solution.py:78
  292.8 2.3 constant_dynamic-update-slice_fusion.2
  304.0 29.1 %add_reduce_fusion.2 = (bf16[64,128,384]{2,1,0:T(8,128)(2,1)S(1)}, bf16[64,128,384]{2,1,0:T(8,128)(2,1)S(1)}) fusion(f32[4,128,384]{2,1,0:T(8,128)S(1)} %get-tuple-element.349, f32[4,64,384]{2,1,0:T(8,128)S(1)} %get-tuple-element.351, f32[4,128,384]{2,1,0:T(8,128)S(1)} %get-tuple-element.352, f32[4,64,384]{2,1,0:T(8,128)S(1)} %get-tuple-element.353), kind=kLoop, calls=%fused_computation.6.clone.1 | loop fusion | flops 94371840 | bytes 14942208 | tf_op jit(solution)/shard_map/while/body/eval_jaxpr/reduce_sum | solution.py:74
  333.1 3.9 %fusion.61 = bf16[8192,256]{1,0:T(8,128)(2,1)S(1)} fusion(bf16[768,256]{1,0:T(8,128)(2,1)S(1)} %get-tuple-element.423, bf16[8192,384]{1,0:T(8,128)(2,1)S(1)} %bitcast.62, bf16[8192,384]{1,0:T(8,128)(2,1)S(1)} %bitcast.61), kind=kOutput, calls=%fused_computation.11.clone.1 | convolution fusion | flops 3248488448 | bytes 17170432 | tf_op jit(solution)/shard_map/while/body/eval_jaxpr/dot_general | solution.py:78
  337.0 2.3 constant_dynamic-update-slice_fusion.2
  (52 shorter events, 22.0 us)
Async XLA Ops:
  6.5 93.9 %all-gather.5.cloned.1.call-start = ((), (), s32[]{:S(2)}) async-start(), calls=%async_computation | async-start | bytes 3538944 | tf_op jit(solution)/shard_map/all_gather | solution.py:101
  7.9 29.1 %collective-permute-start = (bf16[128,4352]{1,0:T(8,128)(2,1)S(1)}, bf16[128,4352]{1,0:T(8,128)(2,1)}, u32[]{:S(2)}, u32[]{:S(2)}) collective-permute-start(bf16[128,4352]{1,0:T(8,128)(2,1)S(1)} %slice.29), channel_id=1, source_target_pairs={{16,0},{17,1},{18,2},{19,3},{20,4},{21,5},{22,6},{23,7},{24,8},{25... | collective-permute-start | bytes 3342344 | tf_op jit(solution)/shard_map/ppermute | solution.py:21
  32.0 5.0 %copy-start = (bf16[128,7680]{1,0:T(8,128)(2,1)S(1)}, bf16[128,7680]{1,0:T(8,128)(2,1)}, u32[]{:S(2)}) copy-start(bf16[128,7680]{1,0:T(8,128)(2,1)} %param.7) | copy-start | bytes 5898244
  32.0 6.4 %copy-start.2 = (s32[4]{0:T(128)S(1)}, s32[4]{0:T(128)}, u32[]{:S(2)}) copy-start(s32[4]{0:T(128)} %param.8) | copy-start | bytes 52
  38.4 124.2 %copy-start.1 = (s32[1,1,4,2]{2,3,1,0:T(2,128)S(1)}, s32[1,1,4,2]{2,3,1,0:T(2,128)}, u32[]{:S(2)}) copy-start(s32[1,1,4,2]{2,3,1,0:T(2,128)} %param.9) | copy-start | bytes 100
  63.3 99.3 %all-gather.7.cloned.1.call-start = ((), (), s32[]{:S(2)}) async-start(), calls=%async_computation.1 | async-start | bytes 3538944 | tf_op jit(solution)/shard_map/all_gather | solution.py:102
Sparse Core Ops, SparseCore 0:
  63.4 36.9 all-gather.4
  102.6 60.0 all-gather.6
where the time goes:
time: 347 us; the launch traced here: 346 us
  other arithmetic  151 us (44%)
  waiting for transfers between devices  97.1 us (28%)
  matrix products  31.3 us (9%)
  loops' own time  27 us (8%)
  local copies, waits for them, and re-layouts  24.2 us (7%)
  between operations  13.5 us (4%)
    reduce_sum x4, other arithmetic, cross_pair(): real_sum = jnp.sum(row_real * col_real + row_imag * col_imag, axis=0)  116 us
    all_gather x1, waiting for transfers between devices, on_device(): col_gathered = lax.all_gather(own_piece, ('tm', 'prow'), axis=0, tiled=True)  62.1 us
    all_gather x1, waiting for transfers between devices, on_device(): row_gathered = lax.all_gather(own_piece, ('tm', 'pcol'), axis=0, tiled=True)  34.4 us
    another operation x1, loops' own time, on_device(): result = lax.map(one_pair, jnp.arange(NP, dtype=jnp.int32))  23.5 us
    dot_general x4, matrix products, cross_pair(): jnp.dot(flat, lags, preferred_element_type=jnp.float32).astype(jnp.bfloat16)  15.7 us
    dot_general x2, matrix products, one_window(): return jnp.dot(segment, dft_table, preferred_element_type=jnp.float32)  14 us
    sub x1, other arithmetic, forward_table(): cos_full = (high_cos * low_cos - high_sin * low_sin).reshape(WIN, NF)  11.8 us
    another operation x2, other arithmetic  11.3 us
  transfers between devices with their start and end apart: 3, of which 2 were waited for; matrix products, arithmetic and copies ran while one was open for 9% of the time, Pallas kernels for 0%

commit v1 on v0

--- a/solution.py
+++ b/solution.py
@@ -99,7 +99,31 @@
     whitened = whiten(spectra)
     own_piece = whitened[None]
     row_gathered = lax.all_gather(own_piece, ("tm", "pcol"), axis=0, tiled=True)
-    col_gathered = lax.all_gather(own_piece, ("tm", "prow"), axis=0, tiled=True)
+    seen_now = jax.lax.psum(1, axis_name=("tm", "prow"))
+    tile_out = jax.lax.axis_index(("tm", "prow"))
+    state_now, block_last, ready = (seen_now, tile_out, own_piece.shape[0])
+    column = [(hop_no, (hop_no + 1) % state_now) for hop_no in range(state_now)]
+    grid = [(hop_no, (hop_no - 1) % state_now) for hop_no in range(state_now)]
+    col_gathered = jnp.zeros(
+        (*own_piece.shape[:0], state_now * ready, *own_piece.shape[0 + 1 :]), own_piece.dtype
+    )
+    col_gathered = lax.dynamic_update_slice_in_dim(
+        col_gathered, own_piece, block_last * ready, axis=0
+    )
+    before = response = own_piece
+    b_next = state_now // 2
+    tick = 1
+    while tick < b_next + 1:
+        before = jax.lax.ppermute(before, axis_name=("tm", "prow"), perm=column)
+        col_gathered = lax.dynamic_update_slice_in_dim(
+            col_gathered, before, (block_last - tick) % state_now * ready, axis=0
+        )
+        if tick < state_now - b_next:
+            response = jax.lax.ppermute(response, axis_name=("tm", "prow"), perm=grid)
+            col_gathered = lax.dynamic_update_slice_in_dim(
+                col_gathered, response, (block_last + tick) % state_now * ready, axis=0
+            )
+        tick += 1
     row_gathered = row_gathered.reshape(n_tm, -1, w_dev, channels_here, 2 * NF)
     col_gathered = col_gathered.reshape(n_tm, -1, w_dev, channels_here, 2 * NF)
     pick_dim = 1

time: 347 us -> 320 us (0.922)
  waiting for transfers between devices: 97.1 us -> 40.3 us
  starting transfers between devices: 1.52 us -> 21 us
  local copies, waits for them, and re-layouts: 24.2 us -> 34.2 us
    all_gather x1 -> x0, waiting for transfers between devices: 62.1 us -> none  [on_device(): col_gathered = lax.all_gather(own_piece, ('tm', 'prow'), axis=0, tiled=True)]
    ppermute x0 -> x7, waiting for transfers between devices: none -> 40.3 us  [the longest x4 33.7 us: on_device(): before = jax.lax.ppermute(before, axis_name=('tm', 'prow'), perm=column)]
    all_gather x1, waiting for transfers between devices: 34.4 us -> 0.02 us  [on_device(): row_gathered = lax.all_gather(own_piece, ('tm', 'pcol'), axis=0, tiled=True)]
    ppermute x0 -> x7, starting transfers between devices: none -> 19.7 us  [the longest x3 16.6 us: on_device(): response = jax.lax.ppermute(response, axis_name=('tm', 'prow'), perm=grid)]
    dynamic_update_slice x0 -> x7, local copies, waits for them, and re-layouts: none -> 5.18 us  [the longest x4 3.1 us: on_device(): lax.dynamic_update_slice_in_dim(col_gathered, before, (block_last - tick)...]
    while x0 -> x24, local copies, waits for them, and re-layouts: none -> 3.97 us
  transfers between devices with their start and end apart: 3 -> 9, of which waited for: 2 -> 7; matrix products, arithmetic and copies ran while one was open for 9% -> 11% of each run, Pallas kernels for 0% -> 0%
where the time goes in v1:
time: 320 us; the launch traced here: 318 us
  other arithmetic  152 us (48%)
  waiting for transfers between devices  40.3 us (13%)
  local copies, waits for them, and re-layouts  34.2 us (11%)
  matrix products  31.3 us (10%)
  loops' own time  25.6 us (8%)
  starting transfers between devices  21 us (7%)
  between operations  13.7 us (4%)
    reduce_sum x4, other arithmetic, cross_pair(): real_sum = jnp.sum(row_real * col_real + row_imag * col_imag, axis=0)  116 us
    ppermute x4, waiting for transfers between devices, on_device(): before = jax.lax.ppermute(before, axis_name=('tm', 'prow'), perm=column)  33.7 us
    another operation x1, loops' own time, on_device(): result = lax.map(one_pair, jnp.arange(NP, dtype=jnp.int32))  21.8 us
    ppermute x3, starting transfers between devices, on_device(): response = jax.lax.ppermute(response, axis_name=('tm', 'prow'), perm=grid)  16.6 us
    dot_general x4, matrix products, cross_pair(): jnp.dot(flat, lags, preferred_element_type=jnp.float32).astype(jnp.bfloat16)  15.7 us
    dot_general x2, matrix products, one_window(): return jnp.dot(segment, dft_table, preferred_element_type=jnp.float32)  13.9 us
    sub x1, other arithmetic, forward_table(): cos_full = (high_cos * low_cos - high_sin * low_sin).reshape(WIN, NF)  11.8 us
    another operation x2, other arithmetic  11.3 us
  transfers between devices with their start and end apart: 9, of which 7 were waited for; matrix products, arithmetic and copies ran while one was open for 11% of the time, Pallas kernels for 0%

profile of v1, /device:TPU:0, one launch (start us, length us, event | category | flops | bytes accessed | tf_op | source)
XLA Modules:
  0.0 318.4 jit_solution(6366023684613794909)
XLA Ops:
  10.8 11.8 %multiply_subtract_fusion = (f32[60,128,384]{2,1,0:T(8,128)}, f32[60,128,384]{2,1,0:T(8,128)}) fusion(f32[128,384]{1,0:T(8,128)S(1)} %get-tuple-element.251, f32[60,384]{1,0:T(8,128)S(1)} %get-tuple-element.249, f32[128,384]{1,0:T(8,128)S(1)} %get-tuple-element.250, f32[60,384]{1,0:T(8,128)S(1)} %get-tuple-element.248), kind=kLoop, calls=%fused_computation.28 | loop fusion | flops 17694720 | bytes 24170496 | tf_op jit(solution)/shard_map/sub | solution.py:35
  22.6 9.4 %fusion.17 = (bf16[7680,384]{1,0:T(8,128)(2,1)S(1)}, bf16[7680,384]{1,0:T(8,128)(2,1)S(1)}) fusion(f32[60,128,384]{2,1,0:T(8,128)} %get-tuple-element.245, f32[7680]{0:T(1024)S(1)} %fusion.46, f32[60,128,384]{2,1,0:T(8,128)} %get-tuple-element.244, f32[7680]{0:T(1024)S(1)} %multiply_subtract_fusion.1), kind=kLoop, calls=%fused_computation.24 | loop fusion | flops 11796480 | bytes 35450880 | tf_op jit(solution)/shard_map/convert.7
  32.0 5.0 %pad_maximum_fusion = bf16[7680,768]{1,0:T(8,128)(2,1)} fusion(bf16[7680,384]{1,0:T(8,128)(2,1)S(1)} %get-tuple-element.252, bf16[7680,384]{1,0:T(8,128)(2,1)S(1)} %get-tuple-element.253), kind=kLoop, calls=%fused_computation.22 | loop fusion | flops 23592960 | bytes 23592960 | tf_op jit(solution)/shard_map/concatenate | solution.py:41
  38.4 20.3 %while.24 = (s32[]{:T(128)}, f32[2,128,768]{2,1,0:T(8,128)}, s32[2]{0:T(128)S(1)}, s32[]{:T(128)}, s32[4]{0:T(128)S(1)}, /*index=5*/bf16[128,12032]{1,0:T(8,128)...) while((s32[]{:T(128)}, f32[2,128,768]{2,1,0:T(8,128)}, ...), condition=%wide.region_1.2_spmd, body=%wide.region_0.1_spmd.sunk | while | flops 1509949440 | bytes 14156537 | solution.py:98
  41.6 7.0 %fusion.59 = f32[2,128,768]{2,1,0:T(8,128)} fusion(f32[2,128,768]{2,1,0:T(8,128)} %get-tuple-element.379, s32[]{:T(128)} %get-tuple-element.378, bf16[7680,768]{1,0:T(8,128)(2,1)} %get-tuple-element.396, bf16[128,12032]{1,0:T(8,128)(2,1)S(1)} %get-tuple-element.395, s32[]{:T(128)S(6)} %select_n.191), kind=kOutput, calls=%fused_computation.3.clone.1 | convolution fusion | flops 1509949440 | bytes 14156292 | tf_op jit(solution)/shard_map/while/body/eval_jaxpr/dot_general | solution.py:96
  51.8 6.9 %fusion.59 = f32[2,128,768]{2,1,0:T(8,128)} fusion(f32[2,128,768]{2,1,0:T(8,128)} %get-tuple-element.379, s32[]{:T(128)} %get-tuple-element.378, bf16[7680,768]{1,0:T(8,128)(2,1)} %get-tuple-element.396, bf16[128,12032]{1,0:T(8,128)(2,1)S(1)} %get-tuple-element.395, s32[]{:T(128)S(6)} %select_n.191), kind=kOutput, calls=%fused_computation.3.clone.1 | convolution fusion | flops 1509949440 | bytes 14156292 | tf_op jit(solution)/shard_map/while/body/eval_jaxpr/dot_general | solution.py:96
  64.0 3.1 collective-permute-start.1
  67.1 5.1 %collective-permute-start.2 = (bf16[1,2,128,768]{3,2,1,0:T(8,128)(2,1)}, bf16[1,2,128,768]{3,2,1,0:T(8,128)(2,1)}, u32[]{:S(2)}, u32[]{:S(2)}) collective-permute-start(bf16[1,2,128,768]{3,2,1,0:T(8,128)(2,1)} %bitcast.71), channel_id=1, source_target_pairs={{0,28},{4,0},{8,4},{12,8},{16,12},{20,16},{24,20},{28,24},{1,29},{... | collective-permute-start | bytes 1179656 | tf_op jit(solution)/shard_map/ppermute | solution.py:122
  72.2 10.2 %collective-permute-done.1 = bf16[1,2,128,768]{3,2,1,0:T(8,128)(2,1)S(1)} collective-permute-done((bf16[1,2,128,768]{3,2,1,0:T(8,128)(2,1)}, bf16[1,2,128,768]{3,2,1,0:T(8,128)(2,1)S(1)}, u32[]{:S(2)}, u32[]{:S(2)}) %collective-permute-start.1) | collective-permute-done | bytes 393248 | tf_op jit(solution)/shard_map/ppermute | solution.py:117
  82.4 4.0 %collective-permute-done.2 = bf16[1,2,128,768]{3,2,1,0:T(8,128)(2,1)} collective-permute-done((bf16[1,2,128,768]{3,2,1,0:T(8,128)(2,1)}, bf16[1,2,128,768]{3,2,1,0:T(8,128)(2,1)}, u32[]{:S(2)}, u32[]{:S(2)}) %collective-permute-start.2) | collective-permute-done | bytes 393248 | tf_op jit(solution)/shard_map/ppermute | solution.py:122
  86.4 4.2 %collective-permute-start.4 = (bf16[1,2,128,768]{3,2,1,0:T(8,128)(2,1)}, bf16[1,2,128,768]{3,2,1,0:T(8,128)(2,1)}, u32[]{:S(2)}, u32[]{:S(2)}) collective-permute-start(bf16[1,2,128,768]{3,2,1,0:T(8,128)(2,1)} %collective-permute-done.2), channel_id=1, source_target_pairs={{0,28},{4,0},{8,4},{12,8},{16,12},{20,16},{24,20},{28,24},{1,29},{... | collective-permute-start | bytes 1179656 | tf_op jit(solution)/shard_map/ppermute | solution.py:122
  90.6 9.9 %collective-permute-done.3 = bf16[1,2,128,768]{3,2,1,0:T(8,128)(2,1)} collective-permute-done((bf16[1,2,128,768]{3,2,1,0:T(8,128)(2,1)S(1)}, bf16[1,2,128,768]{3,2,1,0:T(8,128)(2,1)}, u32[]{:S(2)}, u32[]{:S(2)}) %collective-permute-start.3) | collective-permute-done | bytes 393248 | tf_op jit(solution)/shard_map/ppermute | solution.py:117
  104.8 7.3 %collective-permute-start.6 = (bf16[1,2,128,768]{3,2,1,0:T(8,128)(2,1)}, bf16[1,2,128,768]{3,2,1,0:T(8,128)(2,1)S(1)}, u32[]{:S(2)}, u32[]{:S(2)}) collective-permute-start(bf16[1,2,128,768]{3,2,1,0:T(8,128)(2,1)} %collective-permute-done.4), channel_id=1, source_target_pairs={{0,28},{4,0},{8,4},{12,8},{16,12},{20,16},{24,20},{28,24},{1,29},{... | collective-permute-start | bytes 1179656 | tf_op jit(solution)/shard_map/ppermute | solution.py:122
  113.2 5.3 %collective-permute-done.5 = bf16[1,2,128,768]{3,2,1,0:T(8,128)(2,1)} collective-permute-done((bf16[1,2,128,768]{3,2,1,0:T(8,128)(2,1)}, bf16[1,2,128,768]{3,2,1,0:T(8,128)(2,1)}, u32[]{:S(2)}, u32[]{:S(2)}) %collective-permute-start.5) | collective-permute-done | bytes 393248 | tf_op jit(solution)/shard_map/ppermute | solution.py:117
  123.6 8.4 %collective-permute-done.7 = bf16[1,2,128,768]{3,2,1,0:T(8,128)(2,1)S(1)} collective-permute-done((bf16[1,2,128,768]{3,2,1,0:T(8,128)(2,1)}, bf16[1,2,128,768]{3,2,1,0:T(8,128)(2,1)S(1)}, u32[]{:S(2)}, u32[]{:S(2)}) %collective-permute-start.7) | collective-permute-done | bytes 393248 | tf_op jit(solution)/shard_map/ppermute | solution.py:117
  132.1 179.4 %while.25 = (s32[]{:T(128)}, bf16[4,64,128,256]{3,2,1,0:T(8,128)(2,1)}, s32[4]{0:T(128)S(1)}, s32[4,2]{0,1:T(2,128)S(1)}, bf16[2,4,2,128,768]{4,3,2,1,0:T(8,128)...) while((s32[]{:T(128)}, ...), condition=%wide.region_6.7_spmd, body=%wide.region_3.6_spmd.sunk | while | flops 3343450112 | bytes 73925488 | solution.py:145
  140.6 29.1 %add_reduce_fusion.2 = (bf16[64,128,384]{2,1,0:T(8,128)(2,1)S(1)}, bf16[64,128,384]{2,1,0:T(8,128)(2,1)S(1)}) fusion(f32[4,128,384]{2,1,0:T(8,128)S(1)} %get-tuple-element.359, f32[4,64,384]{2,1,0:T(8,128)S(1)} %get-tuple-element.361, f32[4,128,384]{2,1,0:T(8,128)S(1)} %get-tuple-element.362, f32[4,64,384]{2,1,0:T(8,128)S(1)} %get-tuple-element.363), kind=kLoop, calls=%fused_computation.6.clone.1 | loop fusion | flops 94371840 | bytes 14942208 | tf_op jit(solution)/shard_map/while/body/eval_jaxpr/reduce_sum | solution.py:74
  169.7 3.9 %fusion.62 = bf16[8192,256]{1,0:T(8,128)(2,1)S(1)} fusion(bf16[768,256]{1,0:T(8,128)(2,1)S(1)} %copy-done.3, bf16[8192,384]{1,0:T(8,128)(2,1)S(1)} %bitcast.64, bf16[8192,384]{1,0:T(8,128)(2,1)S(1)} %bitcast.63), kind=kOutput, calls=%fused_computation.11.clone.1 | convolution fusion | flops 3248488448 | bytes 17170432 | tf_op jit(solution)/shard_map/while/body/eval_jaxpr/dot_general | solution.py:78
  185.4 29.1 %add_reduce_fusion.2 = (bf16[64,128,384]{2,1,0:T(8,128)(2,1)S(1)}, bf16[64,128,384]{2,1,0:T(8,128)(2,1)S(1)}) fusion(f32[4,128,384]{2,1,0:T(8,128)S(1)} %get-tuple-element.359, f32[4,64,384]{2,1,0:T(8,128)S(1)} %get-tuple-element.361, f32[4,128,384]{2,1,0:T(8,128)S(1)} %get-tuple-element.362, f32[4,64,384]{2,1,0:T(8,128)S(1)} %get-tuple-element.363), kind=kLoop, calls=%fused_computation.6.clone.1 | loop fusion | flops 94371840 | bytes 14942208 | tf_op jit(solution)/shard_map/while/body/eval_jaxpr/reduce_sum | solution.py:74
  214.5 3.9 %fusion.62 = bf16[8192,256]{1,0:T(8,128)(2,1)S(1)} fusion(bf16[768,256]{1,0:T(8,128)(2,1)S(1)} %copy-done.3, bf16[8192,384]{1,0:T(8,128)(2,1)S(1)} %bitcast.64, bf16[8192,384]{1,0:T(8,128)(2,1)S(1)} %bitcast.63), kind=kOutput, calls=%fused_computation.11.clone.1 | convolution fusion | flops 3248488448 | bytes 17170432 | tf_op jit(solution)/shard_map/while/body/eval_jaxpr/dot_general | solution.py:78
  230.3 29.1 %add_reduce_fusion.2 = (bf16[64,128,384]{2,1,0:T(8,128)(2,1)S(1)}, bf16[64,128,384]{2,1,0:T(8,128)(2,1)S(1)}) fusion(f32[4,128,384]{2,1,0:T(8,128)S(1)} %get-tuple-element.359, f32[4,64,384]{2,1,0:T(8,128)S(1)} %get-tuple-element.361, f32[4,128,384]{2,1,0:T(8,128)S(1)} %get-tuple-element.362, f32[4,64,384]{2,1,0:T(8,128)S(1)} %get-tuple-element.363), kind=kLoop, calls=%fused_computation.6.clone.1 | loop fusion | flops 94371840 | bytes 14942208 | tf_op jit(solution)/shard_map/while/body/eval_jaxpr/reduce_sum | solution.py:74
  259.4 3.9 %fusion.62 = bf16[8192,256]{1,0:T(8,128)(2,1)S(1)} fusion(bf16[768,256]{1,0:T(8,128)(2,1)S(1)} %copy-done.3, bf16[8192,384]{1,0:T(8,128)(2,1)S(1)} %bitcast.64, bf16[8192,384]{1,0:T(8,128)(2,1)S(1)} %bitcast.63), kind=kOutput, calls=%fused_computation.11.clone.1 | convolution fusion | flops 3248488448 | bytes 17170432 | tf_op jit(solution)/shard_map/while/body/eval_jaxpr/dot_general | solution.py:78
  275.1 29.1 %add_reduce_fusion.2 = (bf16[64,128,384]{2,1,0:T(8,128)(2,1)S(1)}, bf16[64,128,384]{2,1,0:T(8,128)(2,1)S(1)}) fusion(f32[4,128,384]{2,1,0:T(8,128)S(1)} %get-tuple-element.359, f32[4,64,384]{2,1,0:T(8,128)S(1)} %get-tuple-element.361, f32[4,128,384]{2,1,0:T(8,128)S(1)} %get-tuple-element.362, f32[4,64,384]{2,1,0:T(8,128)S(1)} %get-tuple-element.363), kind=kLoop, calls=%fused_computation.6.clone.1 | loop fusion | flops 94371840 | bytes 14942208 | tf_op jit(solution)/shard_map/while/body/eval_jaxpr/reduce_sum | solution.py:74
  304.2 3.9 %fusion.62 = bf16[8192,256]{1,0:T(8,128)(2,1)S(1)} fusion(bf16[768,256]{1,0:T(8,128)(2,1)S(1)} %copy-done.3, bf16[8192,384]{1,0:T(8,128)(2,1)S(1)} %bitcast.64, bf16[8192,384]{1,0:T(8,128)(2,1)S(1)} %bitcast.63), kind=kOutput, calls=%fused_computation.11.clone.1 | convolution fusion | flops 3248488448 | bytes 17170432 | tf_op jit(solution)/shard_map/while/body/eval_jaxpr/dot_general | solution.py:78
  (97 shorter events, 49.4 us)
Async XLA Ops:
  6.5 125.6 %all-gather.3.cloned.1.call-start = ((), (), s32[]{:S(2)}) async-start(), calls=%async_computation | async-start | bytes 3538944 | tf_op jit(solution)/shard_map/all_gather | solution.py:101
  7.9 29.1 %collective-permute-start = (bf16[128,4352]{1,0:T(8,128)(2,1)S(1)}, bf16[128,4352]{1,0:T(8,128)(2,1)}, u32[]{:S(2)}, u32[]{:S(2)}) collective-permute-start(bf16[128,4352]{1,0:T(8,128)(2,1)S(1)} %slice.29), channel_id=1, source_target_pairs={{16,0},{17,1},{18,2},{19,3},{20,4},{21,5},{22,6},{23,7},{24,8},{25... | collective-permute-start | bytes 3342344 | tf_op jit(solution)/shard_map/ppermute | solution.py:21
  32.0 5.0 %copy-start.2 = (bf16[128,7680]{1,0:T(8,128)(2,1)S(1)}, bf16[128,7680]{1,0:T(8,128)(2,1)}, u32[]{:S(2)}) copy-start(bf16[128,7680]{1,0:T(8,128)(2,1)} %param.7) | copy-start | bytes 5898244
  32.0 6.4 %copy-start.6 = (s32[4]{0:T(128)S(1)}, s32[4]{0:T(128)}, u32[]{:S(2)}) copy-start(s32[4]{0:T(128)} %param.8) | copy-start | bytes 52
  61.7 70.5 %copy-start.5 = (s32[1,1,4,2]{2,3,1,0:T(2,128)S(1)}, s32[1,1,4,2]{2,3,1,0:T(2,128)}, u32[]{:S(2)}) copy-start(s32[1,1,4,2]{2,3,1,0:T(2,128)} %param.9) | copy-start | bytes 100
  64.0 18.4 %collective-permute-start.1 = (bf16[1,2,128,768]{3,2,1,0:T(8,128)(2,1)}, bf16[1,2,128,768]{3,2,1,0:T(8,128)(2,1)S(1)}, u32[]{:S(2)}, u32[]{:S(2)}) collective-permute-start(bf16[1,2,128,768]{3,2,1,0:T(8,128)(2,1)} %bitcast.70), channel_id=1, source_target_pairs={{0,4},{4,8},{8,12},{12,16},{16,20},{20,24},{24,28},{28,0},{1,5},{5... | collective-permute-start | bytes 1179656 | tf_op jit(solution)/shard_map/ppermute | solution.py:117
  67.1 19.3 %collective-permute-start.2 = (bf16[1,2,128,768]{3,2,1,0:T(8,128)(2,1)}, bf16[1,2,128,768]{3,2,1,0:T(8,128)(2,1)}, u32[]{:S(2)}, u32[]{:S(2)}) collective-permute-start(bf16[1,2,128,768]{3,2,1,0:T(8,128)(2,1)} %bitcast.71), channel_id=1, source_target_pairs={{0,28},{4,0},{8,4},{12,8},{16,12},{20,16},{24,20},{28,24},{1,29},{... | collective-permute-start | bytes 1179656 | tf_op jit(solution)/shard_map/ppermute | solution.py:122
  82.4 18.1 %copy-start.4 = (bf16[1,2,128,768]{3,2,1,0:T(8,128)(2,1)}, bf16[1,2,128,768]{3,2,1,0:T(8,128)(2,1)S(1)}, u32[]{:S(2)}) copy-start(bf16[1,2,128,768]{3,2,1,0:T(8,128)(2,1)S(1)} %collective-permute-done.1) | copy-start | bytes 1179652
  82.4 18.1 %collective-permute-start.3 = (bf16[1,2,128,768]{3,2,1,0:T(8,128)(2,1)S(1)}, bf16[1,2,128,768]{3,2,1,0:T(8,128)(2,1)}, u32[]{:S(2)}, u32[]{:S(2)}) collective-permute-start(bf16[1,2,128,768]{3,2,1,0:T(8,128)(2,1)S(1)} %collective-permute-done.1), channel_id=1, source_target_pairs={{0,4},{4,8},{8,12},{12,16},{16,20},{20,24},{24,28},{28,0},{1,5},{5... | collective-permute-start | bytes 1179656 | tf_op jit(solution)/shard_map/ppermute | solution.py:117
  86.4 18.4 %collective-permute-start.4 = (bf16[1,2,128,768]{3,2,1,0:T(8,128)(2,1)}, bf16[1,2,128,768]{3,2,1,0:T(8,128)(2,1)}, u32[]{:S(2)}, u32[]{:S(2)}) collective-permute-start(bf16[1,2,128,768]{3,2,1,0:T(8,128)(2,1)} %collective-permute-done.2), channel_id=1, source_target_pairs={{0,28},{4,0},{8,4},{12,8},{16,12},{20,16},{24,20},{28,24},{1,29},{... | collective-permute-start | bytes 1179656 | tf_op jit(solution)/shard_map/ppermute | solution.py:122
  100.5 18.0 %collective-permute-start.5 = (bf16[1,2,128,768]{3,2,1,0:T(8,128)(2,1)}, bf16[1,2,128,768]{3,2,1,0:T(8,128)(2,1)}, u32[]{:S(2)}, u32[]{:S(2)}) collective-permute-start(bf16[1,2,128,768]{3,2,1,0:T(8,128)(2,1)} %collective-permute-done.3), channel_id=1, source_target_pairs={{0,4},{4,8},{8,12},{12,16},{16,20},{20,24},{24,28},{28,0},{1,5},{5... | collective-permute-start | bytes 1179656 | tf_op jit(solution)/shard_map/ppermute | solution.py:117
  104.8 18.8 %collective-permute-start.6 = (bf16[1,2,128,768]{3,2,1,0:T(8,128)(2,1)}, bf16[1,2,128,768]{3,2,1,0:T(8,128)(2,1)S(1)}, u32[]{:S(2)}, u32[]{:S(2)}) collective-permute-start(bf16[1,2,128,768]{3,2,1,0:T(8,128)(2,1)} %collective-permute-done.4), channel_id=1, source_target_pairs={{0,28},{4,0},{8,4},{12,8},{16,12},{20,16},{24,20},{28,24},{1,29},{... | collective-permute-start | bytes 1179656 | tf_op jit(solution)/shard_map/ppermute | solution.py:122
  118.4 13.6 %collective-permute-start.7 = (bf16[1,2,128,768]{3,2,1,0:T(8,128)(2,1)}, bf16[1,2,128,768]{3,2,1,0:T(8,128)(2,1)S(1)}, u32[]{:S(2)}, u32[]{:S(2)}) collective-permute-start(bf16[1,2,128,768]{3,2,1,0:T(8,128)(2,1)} %collective-permute-done.5), channel_id=1, source_target_pairs={{0,4},{4,8},{8,12},{12,16},{16,20},{20,24},{24,28},{28,0},{1,5},{5... | collective-permute-start | bytes 1179656 | tf_op jit(solution)/shard_map/ppermute | solution.py:117
  132.1 6.7 %copy-start = (bf16[2,4,2,128,768]{4,3,2,1,0:T(8,128)(2,1)}, bf16[2,4,2,128,768]{4,3,2,1,0:T(8,128)(2,1)S(1)}, u32[]{:S(2)}) copy-start(bf16[2,4,2,128,768]{4,3,2,1,0:T(8,128)(2,1)S(1)} %get-tuple-element.432) | copy-start | bytes 9437188 | tf_op jit(solution)/shard_map/while
  140.5 29.1 %copy-start.3 = (bf16[768,256]{1,0:T(8,128)(2,1)S(1)}, bf16[768,256]{1,0:T(8,128)(2,1)}, u32[]{:S(2)}) copy-start(bf16[768,256]{1,0:T(8,128)(2,1)} %get-tuple-element.433) | copy-start | bytes 1179652 | tf_op jit(solution)/shard_map/while
  173.6 3.4 %copy-start.1 = (bf16[2,4,2,128,768]{4,3,2,1,0:T(8,128)(2,1)S(1)}, bf16[2,4,2,128,768]{4,3,2,1,0:T(8,128)(2,1)}, u32[]{:S(2)}) copy-start(bf16[2,4,2,128,768]{4,3,2,1,0:T(8,128)(2,1)} %copy-done) | copy-start | bytes 9437188 | tf_op jit(solution)/shard_map/while
  177.0 6.7 %copy-start = (bf16[2,4,2,128,768]{4,3,2,1,0:T(8,128)(2,1)}, bf16[2,4,2,128,768]{4,3,2,1,0:T(8,128)(2,1)S(1)}, u32[]{:S(2)}) copy-start(bf16[2,4,2,128,768]{4,3,2,1,0:T(8,128)(2,1)S(1)} %get-tuple-element.432) | copy-start | bytes 9437188 | tf_op jit(solution)/shard_map/while
  185.4 29.1 %copy-start.3 = (bf16[768,256]{1,0:T(8,128)(2,1)S(1)}, bf16[768,256]{1,0:T(8,128)(2,1)}, u32[]{:S(2)}) copy-start(bf16[768,256]{1,0:T(8,128)(2,1)} %get-tuple-element.433) | copy-start | bytes 1179652 | tf_op jit(solution)/shard_map/while
  218.5 3.4 %copy-start.1 = (bf16[2,4,2,128,768]{4,3,2,1,0:T(8,128)(2,1)S(1)}, bf16[2,4,2,128,768]{4,3,2,1,0:T(8,128)(2,1)}, u32[]{:S(2)}) copy-start(bf16[2,4,2,128,768]{4,3,2,1,0:T(8,128)(2,1)} %copy-done) | copy-start | bytes 9437188 | tf_op jit(solution)/shard_map/while
  221.9 6.7 %copy-start = (bf16[2,4,2,128,768]{4,3,2,1,0:T(8,128)(2,1)}, bf16[2,4,2,128,768]{4,3,2,1,0:T(8,128)(2,1)S(1)}, u32[]{:S(2)}) copy-start(bf16[2,4,2,128,768]{4,3,2,1,0:T(8,128)(2,1)S(1)} %get-tuple-element.432) | copy-start | bytes 9437188 | tf_op jit(solution)/shard_map/while
  230.3 29.1 %copy-start.3 = (bf16[768,256]{1,0:T(8,128)(2,1)S(1)}, bf16[768,256]{1,0:T(8,128)(2,1)}, u32[]{:S(2)}) copy-start(bf16[768,256]{1,0:T(8,128)(2,1)} %get-tuple-element.433) | copy-start | bytes 1179652 | tf_op jit(solution)/shard_map/while
  266.7 6.7 %copy-start = (bf16[2,4,2,128,768]{4,3,2,1,0:T(8,128)(2,1)}, bf16[2,4,2,128,768]{4,3,2,1,0:T(8,128)(2,1)S(1)}, u32[]{:S(2)}) copy-start(bf16[2,4,2,128,768]{4,3,2,1,0:T(8,128)(2,1)S(1)} %get-tuple-element.432) | copy-start | bytes 9437188 | tf_op jit(solution)/shard_map/while
  275.1 29.1 %copy-start.3 = (bf16[768,256]{1,0:T(8,128)(2,1)S(1)}, bf16[768,256]{1,0:T(8,128)(2,1)}, u32[]{:S(2)}) copy-start(bf16[768,256]{1,0:T(8,128)(2,1)} %get-tuple-element.433) | copy-start | bytes 1179652 | tf_op jit(solution)/shard_map/while
  308.2 3.4 %copy-start.1 = (bf16[2,4,2,128,768]{4,3,2,1,0:T(8,128)(2,1)S(1)}, bf16[2,4,2,128,768]{4,3,2,1,0:T(8,128)(2,1)}, u32[]{:S(2)}) copy-start(bf16[2,4,2,128,768]{4,3,2,1,0:T(8,128)(2,1)} %copy-done) | copy-start | bytes 9437188 | tf_op jit(solution)/shard_map/while
  (1 other events, 3.4 us)
Sparse Core Ops, SparseCore 0:
  64.1 51.9 all-gather.2
